TPU v7x, 256 devices: a whole 4x4x8 slice. The times are simulated.
256 devices in a mesh: dp: 16 (over z, core), expert: 16 (over x, y).
Axes of the slice: x: 4, y: 4, z: 8, core: 2. Of those that a mesh axis runs over, the one named last changes fastest.
Arguments:
- tokens: bfloat16 [32768, 2048], P(('dp', 'expert')), may hold values from -24 to 24
- cotangent: bfloat16 [32768, 2048], P(('dp', 'expert')), may hold values from -6 to 6
- expert_ids: int32 [32768, 2], P(('dp', 'expert')), may hold values from 0 to 15, all different within a row; in each aligned block of 128 rows (0 to 127, 128 to 255, ...) at most 24 rows name the same one
- placed: int32 [16], replicated, may hold values from 0 to 15, as said below
- router_weight: bfloat16 [2048, 16], replicated, may hold values from -0.125 to 0.125
- gate_weight: bfloat16 [16, 2048, 768], P('expert', 'dp'), may hold values from -0.125 to 0.125
- up_weight: bfloat16 [16, 2048, 768], P('expert', 'dp'), may hold values from -0.125 to 0.125
- down_weight: bfloat16 [16, 2048, 768], P('expert', 'dp'), may hold values from -0.21875 to 0.21875
Outputs:
- mixed: bfloat16 [32768, 2048], P(('dp', 'expert'))
- token_grad: bfloat16 [32768, 2048], P(('dp', 'expert'))
- gate_grad: bfloat16 [16, 2048, 768], P('expert', 'dp')
- up_grad: bfloat16 [16, 2048, 768], P('expert', 'dp')
- down_grad: bfloat16 [16, 2048, 768], P('expert', 'dp')
- router_grad: float32 [2048, 16], replicated
Inputs may be any that keep to these rules, and one draw needn't show every extreme that they name: `expert_ids`: within the rows of one device (128 tokens, two experts each) no expert is named by more than 24 rows, and in some device some expert is named by exactly 24; a token names two different experts. placed is its own inverse, and placed[d] equals d or differs from d in exactly one bit.
All inputs are finite; a program needn't handle non-finite values.
Results may differ from a plain program's by a relative error of at most 0.018.
Values may be sent and summed in bfloat16 or wider, within the bound.
No kernel may reach another device: no remote copies, remote signals or barrier semaphores. Data moves between devices by JAX's collectives and lax.ppermute only.
A program may use at most 128 MiB of HBM per device.

v0:
```python
import jax
import jax.numpy as jnp
from jax import lax
from jax.sharding import PartitionSpec as P
from jax.experimental.layout import Layout, with_layout_constraint


def swapped(array, axis, stride):
    return lax.ppermute(array, axis, [(i, i ^ 1 << stride) for i in range(lax.axis_size(axis))])


def gather_by_exchange(piece, axis):
    count = lax.axis_size(axis)
    copies = jnp.broadcast_to(piece[None], (count,) + piece.shape)
    joined = lax.all_to_all(copies, axis, 0, 0, tiled=True)
    return joined.reshape((count * piece.shape[0],) + piece.shape[1:])


def reduce_router(term, companion, partner, my_index):
    groups = lax.axis_size("expert")
    replicas = lax.axis_size("dp")
    rows = term.shape[0]
    parts = lax.all_to_all(
        term.reshape(groups, rows // groups, term.shape[1]), "expert", 0, 0, tiled=True
    )
    piece = jnp.sum(parts, axis=0)
    piece, companion = lax.optimization_barrier((piece, companion))
    arrivals = [
        swapped(companion, "expert", bit_level) for bit_level in range(groups.bit_length() - 1)
    ]
    for bit_level in range(replicas.bit_length() - 1):
        piece = piece + swapped(piece, "dp", bit_level)
    piece, arrivals = lax.optimization_barrier((piece, arrivals))
    chosen = companion
    for bit_level, arrived in enumerate(arrivals):
        chosen = jnp.where(partner == jnp.bitwise_xor(my_index, 1 << bit_level), arrived, chosen)
    return (gather_by_exchange(piece, "expert"), chosen)


def gate_values(logits, picked):
    scores = jax.nn.sigmoid(logits)
    chosen = jnp.sum(scores[:, None, :] * picked, axis=2)
    return chosen / jnp.sum(chosen, axis=1, keepdims=True)


def slot_numbers(expert_ids, holder, capacity, devices):
    labels = jnp.arange(devices, dtype=jnp.int32)
    member_e = (expert_ids[:, :, None] == labels[None, None, :]).astype(jnp.int32)
    target = jnp.sum(member_e * holder[None, None, :], axis=2)
    flat_target = target.reshape(-1)
    member = (flat_target[:, None] == labels[None, :]).astype(jnp.int32)
    ranking = jnp.sum((jnp.cumsum(member, axis=0) - 1) * member, axis=1)
    return (flat_target * capacity + ranking).reshape(expert_ids.shape)


def scatter_rows(per_pair, slot_index, total):
    flat_rows = per_pair.reshape(-1, per_pair.shape[2])
    empty = jnp.zeros((total, per_pair.shape[2]), per_pair.dtype)
    return empty.at[slot_index.reshape(-1)].set(flat_rows)


def expert_forward(slot_rows, gate_full, up_full, down_full):
    pre_gate = jnp.dot(slot_rows, gate_full, preferred_element_type=jnp.float32)
    pre_up = jnp.dot(slot_rows, up_full, preferred_element_type=jnp.float32)
    hidden = (jax.nn.silu(pre_gate) * pre_up).astype(jnp.bfloat16)
    result = lax.dot_general(
        hidden, down_full, (((1,), (1,)), ((), ())), preferred_element_type=jnp.float32
    )
    return (result.astype(jnp.bfloat16), pre_gate, pre_up, hidden)


def expert_backward(d_out, pre_gate, pre_up, gate_full, up_full, down_full):
    d_hidden = jnp.dot(d_out, down_full, preferred_element_type=jnp.float32)
    sigma = jax.nn.sigmoid(pre_gate)
    d_pre_gate = (d_hidden * pre_up * sigma * (1.0 + pre_gate * (1.0 - sigma))).astype(jnp.bfloat16)
    d_pre_up = (d_hidden * pre_gate * sigma).astype(jnp.bfloat16)
    back_dims = (((1,), (1,)), ((), ()))
    d_rows = lax.dot_general(d_pre_gate, gate_full, back_dims, preferred_element_type=jnp.float32)
    d_rows = d_rows + lax.dot_general(
        d_pre_up, up_full, back_dims, preferred_element_type=jnp.float32
    )
    return (d_rows.astype(jnp.bfloat16), d_pre_gate, d_pre_up)


def row_major(array):
    return with_layout_constraint(array, Layout(major_to_minor=tuple(range(array.ndim))))


def contract_rows(left, right):
    return lax.dot_general(
        left, right, (((0,), (0,)), ((), ())), preferred_element_type=jnp.float32
    )


def on_device(
    tokens, cotangent, expert_ids, placed, router_weight, gate_weight, up_weight, down_weight
):
    count = tokens.shape[0]
    width = tokens.shape[1]
    hid_width = gate_weight.shape[2]
    groups = lax.axis_size("expert")
    replicas = lax.axis_size("dp")
    capacity = 3 * count // groups
    total = groups * capacity
    levels = groups.bit_length() - 1
    my_index = lax.axis_index("expert")
    labels = jnp.arange(groups, dtype=jnp.int32)
    partner = jnp.sum(jnp.where(labels == my_index, placed, 0))
    grad_scale = (2.0 * count * replicas) ** (-0.5)
    router_scale = (1.0 * count * replicas * groups) ** (-0.5)
    logits = jnp.dot(tokens, router_weight, preferred_element_type=jnp.float32)
    picked = (expert_ids[:, :, None] == labels[None, None, :]).astype(jnp.float32)

    def gate_of(values):
        return gate_values(values, picked)

    gate_vals, gate_vjp = jax.vjp(gate_of, logits)
    held = jnp.concatenate([gate_weight, up_weight, down_weight], axis=0)
    gathered = lax.all_gather(held, "dp", axis=1, tiled=True)
    gate_full, up_full, down_full = (gathered[0], gathered[1], gathered[2])
    slot_index = slot_numbers(expert_ids, labels, capacity, groups)
    spread = jnp.broadcast_to(tokens[:, None, :], (count, 2, width))
    outbox = scatter_rows(spread, slot_index, total).reshape(groups, capacity, width)
    received = lax.all_to_all(outbox, "expert", split_axis=0, concat_axis=0, tiled=True)
    item_count = received.shape[1]
    forward_slot_rows = received.reshape(-1, width)
    result, pre_gate, pre_up, hidden = expert_forward(
        forward_slot_rows, gate_full, up_full, down_full
    )
    result, pre_gate, pre_up, hidden, inbox = (
        result.reshape(groups, item_count, width),
        pre_gate.reshape(groups, item_count, hid_width),
        pre_up.reshape(groups, item_count, hid_width),
        hidden.reshape(groups, item_count, hid_width),
        received,
    )
    returned = lax.all_to_all(result, "expert", split_axis=0, concat_axis=0, tiled=True).reshape(
        total, width
    )
    expert_out = returned[slot_index].astype(jnp.float32)
    mixed = jnp.sum(gate_vals[:, :, None] * expert_out, axis=1).astype(jnp.bfloat16)
    cot_wide = cotangent.astype(jnp.float32)
    d_gates = jnp.sum(cot_wide[:, None, :] * expert_out, axis=2)
    d_out = (gate_vals[:, :, None] * cot_wide[:, None, :]).astype(jnp.bfloat16)
    d_outbox = scatter_rows(d_out, slot_index, total).reshape(groups, capacity, width)
    d_inbox = lax.all_to_all(d_outbox, "expert", split_axis=0, concat_axis=0, tiled=True).reshape(
        total, width
    )
    gate_back, up_back, down_back = (gate_full, up_full, down_full)
    slot_rows = inbox.reshape(total, width)
    hidden_rows = hidden.reshape(total, hid_width)
    d_rows, d_pre_gate, d_pre_up = expert_backward(
        d_inbox,
        pre_gate.reshape(total, hid_width),
        pre_up.reshape(total, hid_width),
        gate_back,
        up_back,
        down_back,
    )
    d_returned = lax.all_to_all(
        d_rows.reshape(groups, capacity, width), "expert", split_axis=0, concat_axis=0, tiled=True
    ).reshape(total, width)
    d_expert = jnp.sum(d_returned[slot_index].astype(jnp.float32), axis=1)
    pieces = [
        row_major(contract_rows(slot_rows, jnp.concatenate([d_pre_gate, d_pre_up], axis=1))),
        row_major(contract_rows(d_inbox, hidden_rows)),
    ]
    shares = lax.psum_scatter(
        (jnp.concatenate(pieces, axis=1) * grad_scale).astype(jnp.bfloat16),
        "dp",
        scatter_dimension=0,
        tiled=True,
    ).astype(jnp.float32)
    grad_stack = jnp.stack(
        [shares[:, :hid_width], shares[:, hid_width : 2 * hid_width], shares[:, 2 * hid_width :]],
        axis=0,
    ).astype(jnp.bfloat16)
    d_logits = gate_vjp(d_gates)[0].astype(jnp.bfloat16)
    router_term = contract_rows(tokens, d_logits) * router_scale
    router_grad, grad_stack = reduce_router(router_term, grad_stack, partner, my_index)
    router_back = lax.dot_general(
        d_logits, router_weight, (((1,), (1,)), ((), ())), preferred_element_type=jnp.float32
    )
    token_grad = (d_expert + router_back).astype(jnp.bfloat16)
    return (mixed, token_grad, grad_stack[0:1], grad_stack[1:2], grad_stack[2:3], router_grad)


def solution(mesh):
    in_specs = (
        P(("dp", "expert"), None),
        P(("dp", "expert"), None),
        P(("dp", "expert"), None),
        P(),
        P(),
        P("expert", "dp", None),
        P("expert", "dp", None),
        P("expert", "dp", None),
    )
    out_specs = (
        P(("dp", "expert"), None),
        P(("dp", "expert"), None),
        P("expert", "dp", None),
        P("expert", "dp", None),
        P("expert", "dp", None),
        P(),
    )
    return jax.shard_map(
        on_device, mesh=mesh, in_specs=in_specs, out_specs=out_specs, check_vma=False
    )
```

profile of v0, /device:TPU:1, one launch (start us, length us, event | category | flops | bytes accessed | tf_op | source)
XLA Modules:
  0.0 226.3 jit_solution(6985422025171004675)
XLA Ops:
  15.5 7.7 %all-to-all-start = ((bf16[16,24,2048]{2,1,0:T(8,128)(2,1)}), bf16[16,24,2048]{2,1,0:T(8,128)(2,1)S(1)}, u32[]{:S(2)}, u32[]{:S(2)}) async-start(bf16[16,24,2048]{2,1,0:T(8,128)(2,1)} %bitcast.3), calls=%async_computation | async-start | bytes 3145728 | tf_op jit(solution)/shard_map/all_to_all | solution.py:124
  25.7 3.7 %mul.156 = f32[256,2048]{1,0:T(8,128)} reshape(f32[128,2,2048]{2,1,0:T(2,128)} %mul.155) | data formatting | bytes 4194304 | tf_op jit(solution)/shard_map/mul | solution.py:144
  29.9 4.7 %scatter_custom_fusion.1 = bf16[384,2048]{1,0:T(8,128)(2,1)} fusion(s32[256]{0:T(256)S(1)} %bitcast.89, f32[256,2048]{1,0:T(8,128)} %mul.156, f32[256]{0:T(256)S(1)} %div.42, bf16[]{:T(256)} %constant.16.clone.1), kind=kCustom, calls=%fused_computation.34 | custom fusion | flops 1048576 | bytes 3671042 | tf_op jit(solution)/shard_map/scatter | solution.py:59
  34.6 9.4 %all-to-all-done = bf16[16,24,2048]{2,1,0:T(8,128)(2,1)S(1)} async-done(((bf16[16,24,2048]{2,1,0:T(8,128)(2,1)}), bf16[16,24,2048]{2,1,0:T(8,128)(2,1)S(1)}, u32[]{:S(2)}, u32[]{:S(2)}) %all-to-all-start) | async-done | bytes 1572896 | tf_op jit(solution)/shard_map/all_to_all | solution.py:124
  44.0 5.3 %all-to-all-start.2 = ((bf16[16,24,2048]{2,1,0:T(8,128)(2,1)}), bf16[16,24,2048]{2,1,0:T(8,128)(2,1)S(1)}, u32[]{:S(2)}, u32[]{:S(2)}) async-start(bf16[16,24,2048]{2,1,0:T(8,128)(2,1)} %bitcast.84), calls=%async_computation.2 | async-start | bytes 3145728 | tf_op jit(solution)/shard_map/all_to_all | solution.py:146
  49.5 25.4 %all-gather.2.cloned.1.call-done = bf16[3,2048,768]{2,1,0:T(8,128)(2,1)} async-done(((bf16[3,128,768]{2,1,0:T(8,128)(2,1)}), bf16[3,2048,768]{2,1,0:T(8,128)(2,1)}) %all-gather.2.cloned.1.call-update) | async-done | bytes 9437200 | tf_op jit(solution)/shard_map/all_gather | solution.py:119
  74.9 4.3 %fusion.2 = f32[384,768]{1,0:T(8,128)} fusion(bf16[384,2048]{1,0:T(8,128)(2,1)S(1)} %bitcast.79, bf16[3,2048,768]{2,1,0:T(8,128)(2,1)} %all-gather.2.cloned.1.call-done), kind=kOutput, calls=%fused_computation.12 | convolution fusion | flops 1207959552 | bytes 5898240 | tf_op jit(solution)/shard_map/dot_general | solution.py:63
  79.1 4.3 %fusion.3 = f32[384,768]{1,0:T(8,128)} fusion(bf16[384,2048]{1,0:T(8,128)(2,1)S(1)} %bitcast.80, bf16[3,2048,768]{2,1,0:T(8,128)(2,1)} %all-gather.2.cloned.1.call-done), kind=kOutput, calls=%fused_computation.13 | convolution fusion | flops 1207959552 | bytes 5898240 | tf_op jit(solution)/shard_map/dot_general | solution.py:64
  83.4 4.2 %multiply_convert_fusion.1 = (bf16[384,768]{1,0:T(8,128)(2,1)S(1)}, bf16[384,768]{1,0:T(8,128)(2,1)S(1)}, bf16[384,768]{1,0:T(8,128)(2,1)S(1)}) fusion(f32[384,768]{1,0:T(8,128)} %fusion.2, f32[384,768]{1,0:T(8,128)} %fusion.3, bf16[384,2048]{1,0:T(8,128)(2,1)S(1)} %bitcast.82, bf16[3,2048,768]{2,1,0:T(8,128)(2,1)} %all-gather.2.cloned.1.call-done), kind=kOutput, calls=%fused_computation.25 | convolution fusion | flops 1212678144 | bytes 8847360 | tf_op jit(solution)/shard_map/dot_general | solution.py:73
  89.6 3.5 %fusion.6 = f32[2048,1536]{1,0:T(8,128)S(1)} fusion(bf16[384,2048]{1,0:T(8,128)(2,1)S(1)} %bitcast.81, bf16[384,768]{1,0:T(8,128)(2,1)S(1)} %get-tuple-element.24, bf16[384,768]{1,0:T(8,128)(2,1)S(1)} %get-tuple-element.25), kind=kOutput, calls=%fused_computation.21 | convolution fusion | flops 2418278400 | bytes 15335424 | tf_op jit(solution)/shard_map/dot_general | solution.py:90
  93.1 4.8 %fusion = bf16[2048,2304]{1,0:T(8,128)(2,1)} fusion(f32[2048,768]{1,0:T(8,128)S(1)} %fusion.27, f32[2048,1536]{1,0:T(8,128)S(1)} %fusion.6), kind=kLoop, calls=%fused_computation.5 | loop fusion | flops 14155776 | bytes 28311552 | tf_op jit(solution)/shard_map/convert_element_type | solution.py:169
  99.0 4.5 %convolution_convert_fusion = bf16[384,2048]{1,0:T(8,128)(2,1)} fusion(bf16[384,768]{1,0:T(8,128)(2,1)S(1)} %copy-done.10, bf16[3,2048,768]{2,1,0:T(8,128)(2,1)} %all-gather.2.cloned.1.call-done), kind=kOutput, calls=%fused_computation.10 | convolution fusion | flops 1208745984 | bytes 5308416 | tf_op jit(solution)/shard_map/dot_general | solution.py:66
  103.5 6.7 %all-to-all-start.1 = ((bf16[16,24,2048]{2,1,0:T(8,128)(2,1)}), bf16[16,24,2048]{2,1,0:T(8,128)(2,1)S(1)}, u32[]{:S(2)}, u32[]{:S(2)}) async-start(bf16[16,24,2048]{2,1,0:T(8,128)(2,1)} %bitcast.86), calls=%async_computation.1 | async-start | bytes 3145728 | tf_op jit(solution)/shard_map/all_to_all | solution.py:137
  111.8 5.0 %fusion.1 = f32[384,2048]{1,0:T(8,128)} fusion(bf16[384,768]{1,0:T(8,128)(2,1)S(1)} %copy-done.8, bf16[3,2048,768]{2,1,0:T(8,128)(2,1)} %all-gather.2.cloned.1.call-done), kind=kOutput, calls=%fused_computation.11 | convolution fusion | flops 1207959552 | bytes 6881280 | tf_op jit(solution)/shard_map/dot_general | solution.py:78
  116.8 16.2 %all-to-all-done.1 = bf16[16,24,2048]{2,1,0:T(8,128)(2,1)S(1)} async-done(((bf16[16,24,2048]{2,1,0:T(8,128)(2,1)}), bf16[16,24,2048]{2,1,0:T(8,128)(2,1)S(1)}, u32[]{:S(2)}, u32[]{:S(2)}) %all-to-all-start.1) | async-done | bytes 1572896 | tf_op jit(solution)/shard_map/all_to_all | solution.py:137
  137.8 6.0 %multiply_reduce_fusion = (f32[128,2]{1,0:T(8,128)S(1)}, bf16[128,2048]{1,0:T(8,128)(2,1)}) fusion(f32[128,2,2048]{2,1,0:T(2,128)S(1)} %reshape.213, f32[128,2048]{1,0:T(8,128)} %convert_element_type.54, f32[128,2]{1,0:T(8,128)S(1)} %copy.38), kind=kLoop, calls=%fused_computation.18 | loop fusion | flops 1834752 | bytes 3672064 | tf_op jit(solution)/shard_map/reduce_sum | solution.py:143
  144.9 3.6 %all-to-all-start.4 = ((f32[16,128,16]{1,2,0:T(8,128)}), f32[16,128,16]{1,2,0:T(8,128)S(1)}, u32[]{:S(2)}, u32[]{:S(2)}) async-start(f32[16,128,16]{1,2,0:T(8,128)} %bitcast.76), calls=%async_computation.4 | async-start | bytes 262144 | tf_op jit(solution)/shard_map/all_to_all | solution.py:23
  148.4 5.6 %add_convert_fusion = bf16[384,2048]{1,0:T(8,128)(2,1)} fusion(f32[384,2048]{1,0:T(8,128)} %fusion.1, bf16[384,768]{1,0:T(8,128)(2,1)S(1)} %copy-done.6, bf16[3,2048,768]{2,1,0:T(8,128)(2,1)} %all-gather.2.cloned.1.call-done), kind=kOutput, calls=%fused_computation.9 | convolution fusion | flops 1209532416 | bytes 8454144 | tf_op jit(solution)/shard_map/dot_general | solution.py:79
  155.2 5.5 %all-to-all-start.3 = ((bf16[16,24,2048]{2,1,0:T(8,128)(2,1)}), bf16[16,24,2048]{2,1,0:T(8,128)(2,1)S(1)}, u32[]{:S(2)}, u32[]{:S(2)}) async-start(bf16[16,24,2048]{2,1,0:T(8,128)(2,1)} %bitcast.85), calls=%async_computation.3 | async-start | bytes 3145728 | tf_op jit(solution)/shard_map/all_to_all | solution.py:160
  160.8 6.2 %reduce-scatter.2.cloned.1.call-done = bf16[128,2304]{1,0:T(8,128)(2,1)} async-done(((bf16[2048,2304]{1,0:T(8,128)(2,1)}), bf16[128,2304]{1,0:T(8,128)(2,1)}) %reduce-scatter.2.cloned.1.call-update) | async-done | bytes 589840 | tf_op jit(solution)/shard_map/reduce_scatter | solution.py:168
  176.2 4.3 %collective-permute-start = (f32[128,16]{0,1:T(8,128)S(1)}, f32[128,16]{0,1:T(8,128)S(1)}, u32[]{:S(2)}, u32[]{:S(2)}) collective-permute-start(f32[128,16]{0,1:T(8,128)S(1)} %reduce_sum.123), channel_id=1, source_target_pairs={{0,16},{16,0},{32,48},{48,32},{64,80},{80,64},{96,112},{112,96},{1... | collective-permute-start | bytes 24584 | tf_op jit(solution)/shard_map/ppermute | solution.py:9
  202.7 4.4 %collective-permute-done.5 = bf16[3,128,768]{2,1,0:T(8,128)(2,1)} collective-permute-done((bf16[3,128,768]{2,1,0:T(8,128)(2,1)}, bf16[3,128,768]{2,1,0:T(8,128)(2,1)}, u32[]{:S(2)}, u32[]{:S(2)}) %collective-permute-start.5) | collective-permute-done | bytes 589856 | tf_op jit(solution)/shard_map/ppermute | solution.py:9
  207.7 4.4 %all-to-all-start.5 = ((f32[16,128,16]{1,2,0:T(8,128)}), f32[16,128,16]{1,2,0:T(8,128)S(1)}, u32[]{:S(2)}, u32[]{:S(2)}) async-start(f32[16,128,16]{1,2,0:T(8,128)} %broadcast_in_dim.19), calls=%async_computation.6 | async-start | bytes 262144 | tf_op jit(solution)/shard_map/all_to_all | solution.py:15
  214.1 4.6 %all-to-all-done.5 = f32[16,128,16]{1,2,0:T(8,128)S(1)} async-done(((f32[16,128,16]{1,2,0:T(8,128)}), f32[16,128,16]{1,2,0:T(8,128)S(1)}, u32[]{:S(2)}, u32[]{:S(2)}) %all-to-all-start.5) | async-done | bytes 131104 | tf_op jit(solution)/shard_map/all_to_all | solution.py:15
  (106 shorter events, 55.0 us)
Async XLA Ops:
  7.2 22.2 %copy-start = (bf16[2048,16]{0,1:T(8,128)(2,1)S(1)}, bf16[2048,16]{0,1:T(8,128)(2,1)}, u32[]{:S(2)}) copy-start(bf16[2048,16]{0,1:T(8,128)(2,1)} %param.12) | copy-start | bytes 196612
  7.2 2.2 copy-start.11
  7.2 3.7 %copy-start.1 = (bf16[128,2048]{1,0:T(8,128)(2,1)S(1)}, bf16[128,2048]{1,0:T(8,128)(2,1)}, u32[]{:S(2)}) copy-start(bf16[128,2048]{1,0:T(8,128)(2,1)} %param.8) | copy-start | bytes 1572868
  7.2 67.7 %all-gather.2.cloned.1.call-start = ((), (), s32[]{:S(2)}) async-start(), calls=%async_computation.7 | async-start | bytes 10027008 | tf_op jit(solution)/shard_map/all_gather | solution.py:119
  15.5 7.7 %copy-start.3 = (bf16[128,2048]{1,0:T(8,128)(2,1)S(1)}, bf16[128,2048]{1,0:T(8,128)(2,1)}, u32[]{:S(2)}) copy-start(bf16[128,2048]{1,0:T(8,128)(2,1)} %param.9) | copy-start | bytes 1572868
  15.5 28.4 %all-to-all-start = ((bf16[16,24,2048]{2,1,0:T(8,128)(2,1)}), bf16[16,24,2048]{2,1,0:T(8,128)(2,1)S(1)}, u32[]{:S(2)}, u32[]{:S(2)}) async-start(bf16[16,24,2048]{2,1,0:T(8,128)(2,1)} %bitcast.3), calls=%async_computation | async-start | bytes 3145728 | tf_op jit(solution)/shard_map/all_to_all | solution.py:124
  44.0 39.5 %all-to-all-start.2 = ((bf16[16,24,2048]{2,1,0:T(8,128)(2,1)}), bf16[16,24,2048]{2,1,0:T(8,128)(2,1)S(1)}, u32[]{:S(2)}, u32[]{:S(2)}) async-start(bf16[16,24,2048]{2,1,0:T(8,128)(2,1)} %bitcast.84), calls=%async_computation.2 | async-start | bytes 3145728 | tf_op jit(solution)/shard_map/all_to_all | solution.py:146
  49.3 117.7 %reduce-scatter.2.cloned.1.call-start = ((), (), s32[]{:S(2)}) async-start(), calls=%async_computation.8 | async-start | bytes 10027008 | tf_op jit(solution)/shard_map/reduce_scatter | solution.py:168
  103.5 6.8 %copy-start.4 = (bf16[128,2048]{1,0:T(8,128)(2,1)S(1)}, bf16[128,2048]{1,0:T(8,128)(2,1)}, u32[]{:S(2)}) copy-start(bf16[128,2048]{1,0:T(8,128)(2,1)} %param.9) | copy-start | bytes 1572868
  103.5 29.5 %all-to-all-start.1 = ((bf16[16,24,2048]{2,1,0:T(8,128)(2,1)}), bf16[16,24,2048]{2,1,0:T(8,128)(2,1)S(1)}, u32[]{:S(2)}, u32[]{:S(2)}) async-start(bf16[16,24,2048]{2,1,0:T(8,128)(2,1)} %bitcast.86), calls=%async_computation.1 | async-start | bytes 3145728 | tf_op jit(solution)/shard_map/all_to_all | solution.py:137
  137.8 6.2 %copy-start.2 = (bf16[128,2048]{1,0:T(8,128)(2,1)S(1)}, bf16[128,2048]{1,0:T(8,128)(2,1)}, u32[]{:S(2)}) copy-start(bf16[128,2048]{1,0:T(8,128)(2,1)} %param.8) | copy-start | bytes 1572868
  137.8 10.7 %copy-start.6 = (bf16[384,768]{1,0:T(8,128)(2,1)S(1)}, bf16[384,768]{1,0:T(8,128)(2,1)}, u32[]{:S(2)}) copy-start(bf16[384,768]{1,0:T(8,128)(2,1)} %copy-done.5) | copy-start | bytes 1769476
  144.9 10.4 %all-to-all-start.4 = ((f32[16,128,16]{1,2,0:T(8,128)}), f32[16,128,16]{1,2,0:T(8,128)S(1)}, u32[]{:S(2)}, u32[]{:S(2)}) async-start(f32[16,128,16]{1,2,0:T(8,128)} %bitcast.76), calls=%async_computation.4 | async-start | bytes 262144 | tf_op jit(solution)/shard_map/all_to_all | solution.py:23
  155.2 33.4 %all-to-all-start.3 = ((bf16[16,24,2048]{2,1,0:T(8,128)(2,1)}), bf16[16,24,2048]{2,1,0:T(8,128)(2,1)S(1)}, u32[]{:S(2)}, u32[]{:S(2)}) async-start(bf16[16,24,2048]{2,1,0:T(8,128)(2,1)} %bitcast.85), calls=%async_computation.3 | async-start | bytes 3145728 | tf_op jit(solution)/shard_map/all_to_all | solution.py:160
  160.7 24.7 %copy-start.12 = (s32[16]{0:T(128)S(1)}, s32[16]{0:T(128)}, u32[]{:S(2)}) copy-start(s32[16]{0:T(128)} %param.11) | copy-start | bytes 196
  169.0 33.6 %collective-permute-start.4 = (bf16[3,128,768]{2,1,0:T(8,128)(2,1)}, bf16[3,128,768]{2,1,0:T(8,128)(2,1)}, u32[]{:S(2)}, u32[]{:S(2)}) collective-permute-start(bf16[3,128,768]{2,1,0:T(8,128)(2,1)} %pad_maximum_fusion.1), channel_id=1, source_target_pairs={{0,1},{1,0},{2,3},{3,2},{4,5},{5,4},{6,7},{7,6},{8,9},{9,8},{10,11... | collective-permute-start | bytes 1769480 | tf_op jit(solution)/shard_map/ppermute | solution.py:9
  170.3 36.7 %collective-permute-start.5 = (bf16[3,128,768]{2,1,0:T(8,128)(2,1)}, bf16[3,128,768]{2,1,0:T(8,128)(2,1)}, u32[]{:S(2)}, u32[]{:S(2)}) collective-permute-start(bf16[3,128,768]{2,1,0:T(8,128)(2,1)} %pad_maximum_fusion.1), channel_id=1, source_target_pairs={{0,2},{1,3},{2,0},{3,1},{4,6},{5,7},{6,4},{7,5},{8,10},{9,11},{10,... | collective-permute-start | bytes 1769480 | tf_op jit(solution)/shard_map/ppermute | solution.py:9
  172.5 34.5 %collective-permute-start.6 = (bf16[3,128,768]{2,1,0:T(8,128)(2,1)}, bf16[3,128,768]{2,1,0:T(8,128)(2,1)}, u32[]{:S(2)}, u32[]{:S(2)}) collective-permute-start(bf16[3,128,768]{2,1,0:T(8,128)(2,1)} %pad_maximum_fusion.1), channel_id=1, source_target_pairs={{0,4},{1,5},{2,6},{3,7},{4,0},{5,1},{6,2},{7,3},{8,12},{9,13},{10,... | collective-permute-start | bytes 1769480 | tf_op jit(solution)/shard_map/ppermute | solution.py:9
  173.7 33.4 %collective-permute-start.7 = (bf16[3,128,768]{2,1,0:T(8,128)(2,1)}, bf16[3,128,768]{2,1,0:T(8,128)(2,1)}, u32[]{:S(2)}, u32[]{:S(2)}) collective-permute-start(bf16[3,128,768]{2,1,0:T(8,128)(2,1)} %pad_maximum_fusion.1), channel_id=1, source_target_pairs={{0,8},{1,9},{2,10},{3,11},{4,12},{5,13},{6,14},{7,15},{8,0},{9,1},... | collective-permute-start | bytes 1769480 | tf_op jit(solution)/shard_map/ppermute | solution.py:9
  176.2 5.1 %collective-permute-start = (f32[128,16]{0,1:T(8,128)S(1)}, f32[128,16]{0,1:T(8,128)S(1)}, u32[]{:S(2)}, u32[]{:S(2)}) collective-permute-start(f32[128,16]{0,1:T(8,128)S(1)} %reduce_sum.123), channel_id=1, source_target_pairs={{0,16},{16,0},{32,48},{48,32},{64,80},{80,64},{96,112},{112,96},{1... | collective-permute-start | bytes 24584 | tf_op jit(solution)/shard_map/ppermute | solution.py:9
  181.3 2.9 %collective-permute-start.1 = (f32[128,16]{0,1:T(8,128)S(1)}, f32[128,16]{0,1:T(8,128)S(1)}, u32[]{:S(2)}, u32[]{:S(2)}) collective-permute-start(f32[128,16]{0,1:T(8,128)S(1)} %add.85), channel_id=1, source_target_pairs={{0,32},{16,48},{32,0},{48,16},{64,96},{80,112},{96,64},{112,80},{1... | collective-permute-start | bytes 24584 | tf_op jit(solution)/shard_map/ppermute | solution.py:9
  184.2 11.9 %collective-permute-start.2 = (f32[128,16]{0,1:T(8,128)S(1)}, f32[128,16]{0,1:T(8,128)S(1)}, u32[]{:S(2)}, u32[]{:S(2)}) collective-permute-start(f32[128,16]{0,1:T(8,128)S(1)} %add.86), channel_id=1, source_target_pairs={{0,64},{16,80},{32,96},{48,112},{64,0},{80,16},{96,32},{112,48},{1... | collective-permute-start | bytes 24584 | tf_op jit(solution)/shard_map/ppermute | solution.py:9
  196.2 6.5 %collective-permute-start.3 = (f32[128,16]{0,1:T(8,128)S(1)}, f32[128,16]{0,1:T(8,128)S(1)}, u32[]{:S(2)}, u32[]{:S(2)}) collective-permute-start(f32[128,16]{0,1:T(8,128)S(1)} %add.87), channel_id=1, source_target_pairs={{0,128},{16,144},{32,160},{48,176},{64,192},{80,208},{96,224},{112... | collective-permute-start | bytes 24584 | tf_op jit(solution)/shard_map/ppermute | solution.py:9
  207.7 11.1 %all-to-all-start.5 = ((f32[16,128,16]{1,2,0:T(8,128)}), f32[16,128,16]{1,2,0:T(8,128)S(1)}, u32[]{:S(2)}, u32[]{:S(2)}) async-start(f32[16,128,16]{1,2,0:T(8,128)} %broadcast_in_dim.19), calls=%async_computation.6 | async-start | bytes 262144 | tf_op jit(solution)/shard_map/all_to_all | solution.py:15
  (5 other events, 8.3 us)
Sparse Core Ops, SparseCore 0:
  9.9 64.9 all-gather.1
  98.1 68.8 reduce-scatter.1
where the time goes:
time: 227 us; the launch traced here: 226 us
  waiting for transfers between devices  73.9 us (33%)
  starting transfers between devices  48.5 us (21%)
  matrix products  34.8 us (15%)
  local copies, waits for them, and re-layouts  26.8 us (12%)
  other arithmetic  25.1 us (11%)
  between operations  17.1 us (8%)
    all_gather x1, waiting for transfers between devices, on_device(): gathered = lax.all_gather(held, 'dp', axis=1, tiled=True)  25.4 us
    all_to_all x1, waiting for transfers between devices, on_device(): lax.all_to_all(result, 'expert', split_axis=0, concat_axis=0, tiled=True)  16.2 us
    ppermute x8, starting transfers between devices, swapped(): lax.ppermute(array, axis, [(i, i ^ 1 << stride) for i in range(lax.axis_s...  15.1 us
    ppermute x8, waiting for transfers between devices, swapped(): lax.ppermute(array, axis, [(i, i ^ 1 << stride) for i in range(lax.axis_s...  11 us
    all_to_all x1, waiting for transfers between devices, on_device(): lax.all_to_all(outbox, 'expert', split_axis=0, concat_axis=0, tiled=True)  9.37 us
    all_to_all x1, starting transfers between devices, on_device(): lax.all_to_all(outbox, 'expert', split_axis=0, concat_axis=0, tiled=True)  7.7 us
    all_to_all x1, starting transfers between devices, on_device(): lax.all_to_all(result, 'expert', split_axis=0, concat_axis=0, tiled=True)  6.67 us
    reduce_scatter x1, waiting for transfers between devices, on_device(): lax.psum_scatter((jnp.concatenate(pieces, axis=1) * grad_scale).astype(jn...  6.22 us
  transfers between devices with their start and end apart: 16, of which 10 were waited for; matrix products, arithmetic and copies ran while one was open for 30% of the time, Pallas kernels for 0%

commit v1 on v0

--- a/solution.py
+++ b/solution.py
@@ -116,7 +116,9 @@
 
     gate_vals, gate_vjp = jax.vjp(gate_of, logits)
     held = jnp.concatenate([gate_weight, up_weight, down_weight], axis=0)
-    gathered = lax.all_gather(held, "dp", axis=1, tiled=True)
+    gathered = jnp.concatenate(
+        lax.all_to_all(jnp.stack([held] * lax.axis_size("dp"), 0), "dp", 0, 0), 1
+    )
     gate_full, up_full, down_full = (gathered[0], gathered[1], gathered[2])
     slot_index = slot_numbers(expert_ids, labels, capacity, groups)
     spread = jnp.broadcast_to(tokens[:, None, :], (count, 2, width))

time: 227 us -> 441 us (1.94)
  the two profiles are of different devices: /device:TPU:1 before, /device:TPU:96 now
where the time goes in v1:
time: 441 us; the launch traced here: 433 us
  waiting for transfers between devices  272 us (62%)
  starting transfers between devices  50.4 us (11%)
  local copies, waits for them, and re-layouts  38.8 us (9%)
  matrix products  30.8 us (7%)
  other arithmetic  23.8 us (5%)
  between operations  17.3 us (4%)
    all_to_all x1, waiting for transfers between devices, on_device(): lax.all_to_all(jnp.stack([held] * lax.axis_size('dp'), 0), 'dp', 0, 0)  195 us
    all_to_all x1, waiting for transfers between devices, on_device(): lax.all_to_all(outbox, 'expert', split_axis=0, concat_axis=0, tiled=True)  23.7 us
    all_to_all x1, waiting for transfers between devices, on_device(): lax.all_to_all(result, 'expert', split_axis=0, concat_axis=0, tiled=True)  15.5 us
    ppermute x8, starting transfers between devices, swapped(): lax.ppermute(array, axis, [(i, i ^ 1 << stride) for i in range(lax.axis_s...  15 us
    all_to_all x1, waiting for transfers between devices, on_device(): lax.all_to_all(d_outbox, 'expert', split_axis=0, concat_axis=0, tiled=True)  13.1 us
    ppermute x8, waiting for transfers between devices, swapped(): lax.ppermute(array, axis, [(i, i ^ 1 << stride) for i in range(lax.axis_s...  11.3 us
  transfers between devices with their start and end apart: 16, of which 11 were waited for; matrix products, arithmetic and copies ran while one was open for 15% of the time, Pallas kernels for 0%

profile of v1, /device:TPU:96, one launch (start us, length us, event | category | flops | bytes accessed | tf_op | source)
XLA Modules:
  0.0 433.5 jit_solution(15214440058266683133)
XLA Ops:
  15.1 7.2 %all-to-all-start = ((bf16[16,24,2048]{2,1,0:T(8,128)(2,1)}), bf16[16,24,2048]{2,1,0:T(8,128)(2,1)S(1)}, u32[]{:S(2)}, u32[]{:S(2)}) async-start(bf16[16,24,2048]{2,1,0:T(8,128)(2,1)} %bitcast.3), calls=%async_computation | async-start | bytes 3145728 | tf_op jit(solution)/shard_map/all_to_all | solution.py:126
  22.4 23.7 %all-to-all-done = bf16[16,24,2048]{2,1,0:T(8,128)(2,1)S(1)} async-done(((bf16[16,24,2048]{2,1,0:T(8,128)(2,1)}), bf16[16,24,2048]{2,1,0:T(8,128)(2,1)S(1)}, u32[]{:S(2)}, u32[]{:S(2)}) %all-to-all-start) | async-done | bytes 1572896 | tf_op jit(solution)/shard_map/all_to_all | solution.py:126
  46.0 4.8 %stack.14 = bf16[16,3,128,768]{3,2,1,0:T(8,128)(2,1)} broadcast(bf16[3,128,768]{2,1,0:T(8,128)(2,1)S(1)} %pad_maximum_fusion), dimensions={1,2,3} | broadcast | bytes 10027008 | tf_op jit(solution)/shard_map/stack | solution.py:120
  50.8 7.8 %all-to-all-start.1 = ((bf16[16,3,128,768]{3,2,1,0:T(8,128)(2,1)}), bf16[16,3,128,768]{3,2,1,0:T(8,128)(2,1)}, u32[]{:S(2)}, u32[]{:S(2)}) async-start(bf16[16,3,128,768]{3,2,1,0:T(8,128)(2,1)} %stack.14), calls=%async_computation.1 | async-start | bytes 18874368 | tf_op jit(solution)/shard_map/all_to_all | solution.py:120
  61.0 3.7 mul.156
  65.3 4.6 %scatter_custom_fusion.1 = bf16[384,2048]{1,0:T(8,128)(2,1)} fusion(s32[256]{0:T(256)S(1)} %bitcast.91, f32[256,2048]{1,0:T(8,128)} %mul.156, f32[256]{0:T(256)S(1)} %div.42, bf16[]{:T(256)} %constant.16.clone.1), kind=kCustom, calls=%fused_computation.27 | custom fusion | flops 1048576 | bytes 3671042 | tf_op jit(solution)/shard_map/scatter | solution.py:59
  69.9 194.8 %all-to-all-done.1 = bf16[16,3,128,768]{3,2,1,0:T(8,128)(2,1)} async-done(((bf16[16,3,128,768]{3,2,1,0:T(8,128)(2,1)}), bf16[16,3,128,768]{3,2,1,0:T(8,128)(2,1)}, u32[]{:S(2)}, u32[]{:S(2)}) %all-to-all-start.1) | async-done | bytes 9437216 | tf_op jit(solution)/shard_map/all_to_all | solution.py:120
  264.7 3.9 all-to-all-start.3
  269.1 5.4 %fusion.22 = (bf16[1,16,128,768]{3,2,0,1:T(8,128)(2,1)}, bf16[1,16,128,768]{3,2,0,1:T(8,128)(2,1)S(1)}, bf16[1,16,128,768]{3,2,0,1:T(8,128)(2,1)S(1)}) fusion(bf16[3,16,128,768]{3,2,0,1:T(8,128)(2,1)} %bitcast.5), kind=kLoop, calls=%fused_computation.68 | loop fusion | bytes 18874368 | tf_op jit(solution)/shard_map/slice | solution.py:122
  279.9 13.1 %all-to-all-done.3 = bf16[16,24,2048]{2,1,0:T(8,128)(2,1)S(1)} async-done(((bf16[16,24,2048]{2,1,0:T(8,128)(2,1)}), bf16[16,24,2048]{2,1,0:T(8,128)(2,1)S(1)}, u32[]{:S(2)}, u32[]{:S(2)}) %all-to-all-start.3) | async-done | bytes 1572896 | tf_op jit(solution)/shard_map/all_to_all | solution.py:148
  293.0 4.2 multiply_convert_fusion.1
  302.6 4.9 %fusion = bf16[2048,2304]{1,0:T(8,128)(2,1)} fusion(f32[2048,768]{1,0:T(8,128)S(1)} %fusion.27, f32[2048,1536]{1,0:T(8,128)S(1)} %fusion.2), kind=kLoop, calls=%fused_computation.5 | loop fusion | flops 14155776 | bytes 28311552 | tf_op jit(solution)/shard_map/convert_element_type | solution.py:171
  309.5 3.6 convolution_convert_fusion
  313.1 4.0 all-to-all-start.2
  318.7 5.0 %fusion.26 = f32[384,2048]{1,0:T(8,128)} fusion(bf16[384,768]{1,0:T(8,128)(2,1)S(1)} %copy-done.11, bf16[2048,768]{1,0:T(8,128)(2,1)} %bitcast.84), kind=kOutput, calls=%fused_computation.72 | convolution fusion | flops 1207959552 | bytes 6881280 | tf_op jit(solution)/shard_map/dot_general | solution.py:78
  323.8 15.5 %all-to-all-done.2 = bf16[16,24,2048]{2,1,0:T(8,128)(2,1)S(1)} async-done(((bf16[16,24,2048]{2,1,0:T(8,128)(2,1)}), bf16[16,24,2048]{2,1,0:T(8,128)(2,1)S(1)}, u32[]{:S(2)}, u32[]{:S(2)}) %all-to-all-start.2) | async-done | bytes 1572896 | tf_op jit(solution)/shard_map/all_to_all | solution.py:139
  344.1 6.0 %multiply_reduce_fusion = (f32[128,2]{1,0:T(8,128)S(1)}, bf16[128,2048]{1,0:T(8,128)(2,1)}) fusion(f32[128,2,2048]{2,1,0:T(2,128)S(1)} %reshape.226, f32[128,2048]{1,0:T(8,128)} %convert_element_type.54, f32[128,2]{1,0:T(8,128)S(1)} %copy.38), kind=kLoop, calls=%fused_computation.11 | loop fusion | flops 1834752 | bytes 3672064 | tf_op jit(solution)/shard_map/reduce_sum | solution.py:145
  351.1 3.5 all-to-all-start.5
  354.6 5.6 %add_convert_fusion = bf16[384,2048]{1,0:T(8,128)(2,1)} fusion(f32[384,2048]{1,0:T(8,128)} %fusion.26, bf16[384,768]{1,0:T(8,128)(2,1)S(1)} %copy-done.9, bf16[2048,768]{1,0:T(8,128)(2,1)} %bitcast.82), kind=kOutput, calls=%fused_computation.6 | convolution fusion | flops 1209532416 | bytes 8454144 | tf_op jit(solution)/shard_map/dot_general | solution.py:79
  362.4 5.0 %all-to-all-start.4 = ((bf16[16,24,2048]{2,1,0:T(8,128)(2,1)}), bf16[16,24,2048]{2,1,0:T(8,128)(2,1)S(1)}, u32[]{:S(2)}, u32[]{:S(2)}) async-start(bf16[16,24,2048]{2,1,0:T(8,128)(2,1)} %bitcast.87), calls=%async_computation.4 | async-start | bytes 3145728 | tf_op jit(solution)/shard_map/all_to_all | solution.py:162
  367.5 6.0 %reduce-scatter.2.cloned.1.call-done = bf16[128,2304]{1,0:T(8,128)(2,1)} async-done(((bf16[2048,2304]{1,0:T(8,128)(2,1)}), bf16[128,2304]{1,0:T(8,128)(2,1)}) %reduce-scatter.2.cloned.1.call-update) | async-done | bytes 589840 | tf_op jit(solution)/shard_map/reduce_scatter | solution.py:170
  387.1 3.6 collective-permute-done.1
  409.9 3.8 collective-permute-done.5
  420.0 5.7 %all-to-all-done.6 = f32[16,128,16]{1,2,0:T(8,128)S(1)} async-done(((f32[16,128,16]{1,2,0:T(8,128)}), f32[16,128,16]{1,2,0:T(8,128)S(1)}, u32[]{:S(2)}, u32[]{:S(2)}) %all-to-all-start.6) | async-done | bytes 131104 | tf_op jit(solution)/shard_map/all_to_all | solution.py:15
  (117 shorter events, 70.5 us)
Async XLA Ops:
  7.2 57.6 %copy-start = (bf16[2048,16]{0,1:T(8,128)(2,1)S(1)}, bf16[2048,16]{0,1:T(8,128)(2,1)}, u32[]{:S(2)}) copy-start(bf16[2048,16]{0,1:T(8,128)(2,1)} %param.12) | copy-start | bytes 196612
  15.1 7.2 %copy-start.13 = (bf16[1,128,768]{2,1,0:T(8,128)(2,1)S(1)}, bf16[1,128,768]{2,1,0:T(8,128)(2,1)}, u32[]{:S(2)}) copy-start(bf16[1,128,768]{2,1,0:T(8,128)(2,1)} %param.15) | copy-start | bytes 589828
  15.1 7.2 %copy-start.14 = (bf16[1,128,768]{2,1,0:T(8,128)(2,1)S(1)}, bf16[1,128,768]{2,1,0:T(8,128)(2,1)}, u32[]{:S(2)}) copy-start(bf16[1,128,768]{2,1,0:T(8,128)(2,1)} %param.14) | copy-start | bytes 589828
  15.1 7.2 %copy-start.15 = (bf16[1,128,768]{2,1,0:T(8,128)(2,1)S(1)}, bf16[1,128,768]{2,1,0:T(8,128)(2,1)}, u32[]{:S(2)}) copy-start(bf16[1,128,768]{2,1,0:T(8,128)(2,1)} %param.13) | copy-start | bytes 589828
  15.1 31.0 %all-to-all-start = ((bf16[16,24,2048]{2,1,0:T(8,128)(2,1)}), bf16[16,24,2048]{2,1,0:T(8,128)(2,1)S(1)}, u32[]{:S(2)}, u32[]{:S(2)}) async-start(bf16[16,24,2048]{2,1,0:T(8,128)(2,1)} %bitcast.3), calls=%async_computation | async-start | bytes 3145728 | tf_op jit(solution)/shard_map/all_to_all | solution.py:126
  50.8 7.8 %copy-start.6 = (bf16[128,2048]{1,0:T(8,128)(2,1)S(1)}, bf16[128,2048]{1,0:T(8,128)(2,1)}, u32[]{:S(2)}) copy-start(bf16[128,2048]{1,0:T(8,128)(2,1)} %param.9) | copy-start | bytes 1572868
  50.8 213.9 %all-to-all-start.1 = ((bf16[16,3,128,768]{3,2,1,0:T(8,128)(2,1)}), bf16[16,3,128,768]{3,2,1,0:T(8,128)(2,1)}, u32[]{:S(2)}, u32[]{:S(2)}) async-start(bf16[16,3,128,768]{3,2,1,0:T(8,128)(2,1)} %stack.14), calls=%async_computation.1 | async-start | bytes 18874368 | tf_op jit(solution)/shard_map/all_to_all | solution.py:120
  264.7 28.3 %all-to-all-start.3 = ((bf16[16,24,2048]{2,1,0:T(8,128)(2,1)}), bf16[16,24,2048]{2,1,0:T(8,128)(2,1)S(1)}, u32[]{:S(2)}, u32[]{:S(2)}) async-start(bf16[16,24,2048]{2,1,0:T(8,128)(2,1)} %bitcast.80), calls=%async_computation.3 | async-start | bytes 3145728 | tf_op jit(solution)/shard_map/all_to_all | solution.py:148
  268.6 104.9 %reduce-scatter.2.cloned.1.call-start = ((), (), s32[]{:S(2)}) async-start(), calls=%async_computation.8 | async-start | bytes 10027008 | tf_op jit(solution)/shard_map/reduce_scatter | solution.py:170
  313.1 26.2 %all-to-all-start.2 = ((bf16[16,24,2048]{2,1,0:T(8,128)(2,1)}), bf16[16,24,2048]{2,1,0:T(8,128)(2,1)S(1)}, u32[]{:S(2)}, u32[]{:S(2)}) async-start(bf16[16,24,2048]{2,1,0:T(8,128)(2,1)} %bitcast.88), calls=%async_computation.2 | async-start | bytes 3145728 | tf_op jit(solution)/shard_map/all_to_all | solution.py:139
  344.0 6.2 %copy-start.2 = (bf16[128,2048]{1,0:T(8,128)(2,1)S(1)}, bf16[128,2048]{1,0:T(8,128)(2,1)}, u32[]{:S(2)}) copy-start(bf16[128,2048]{1,0:T(8,128)(2,1)} %param.8) | copy-start | bytes 1572868
  344.0 10.6 %copy-start.9 = (bf16[384,768]{1,0:T(8,128)(2,1)S(1)}, bf16[384,768]{1,0:T(8,128)(2,1)}, u32[]{:S(2)}) copy-start(bf16[384,768]{1,0:T(8,128)(2,1)} %copy-done.8) | copy-start | bytes 1769476
  351.1 11.3 %all-to-all-start.5 = ((f32[16,128,16]{1,2,0:T(8,128)}), f32[16,128,16]{1,2,0:T(8,128)S(1)}, u32[]{:S(2)}, u32[]{:S(2)}) async-start(f32[16,128,16]{1,2,0:T(8,128)} %bitcast.72), calls=%async_computation.5 | async-start | bytes 262144 | tf_op jit(solution)/shard_map/all_to_all | solution.py:23
  362.4 32.4 %all-to-all-start.4 = ((bf16[16,24,2048]{2,1,0:T(8,128)(2,1)}), bf16[16,24,2048]{2,1,0:T(8,128)(2,1)S(1)}, u32[]{:S(2)}, u32[]{:S(2)}) async-start(bf16[16,24,2048]{2,1,0:T(8,128)(2,1)} %bitcast.87), calls=%async_computation.4 | async-start | bytes 3145728 | tf_op jit(solution)/shard_map/all_to_all | solution.py:162
  367.4 24.1 %copy-start.17 = (s32[16]{0:T(128)S(1)}, s32[16]{0:T(128)}, u32[]{:S(2)}) copy-start(s32[16]{0:T(128)} %param.11) | copy-start | bytes 196
  375.6 34.4 %collective-permute-start.4 = (bf16[3,128,768]{2,1,0:T(8,128)(2,1)}, bf16[3,128,768]{2,1,0:T(8,128)(2,1)}, u32[]{:S(2)}, u32[]{:S(2)}) collective-permute-start(bf16[3,128,768]{2,1,0:T(8,128)(2,1)} %pad_maximum_fusion.1), channel_id=1, source_target_pairs={{0,1},{1,0},{2,3},{3,2},{4,5},{5,4},{6,7},{7,6},{8,9},{9,8},{10,11... | collective-permute-start | bytes 1769480 | tf_op jit(solution)/shard_map/ppermute | solution.py:9
  377.0 36.8 %collective-permute-start.5 = (bf16[3,128,768]{2,1,0:T(8,128)(2,1)}, bf16[3,128,768]{2,1,0:T(8,128)(2,1)}, u32[]{:S(2)}, u32[]{:S(2)}) collective-permute-start(bf16[3,128,768]{2,1,0:T(8,128)(2,1)} %pad_maximum_fusion.1), channel_id=1, source_target_pairs={{0,2},{1,3},{2,0},{3,1},{4,6},{5,7},{6,4},{7,5},{8,10},{9,11},{10,... | collective-permute-start | bytes 1769480 | tf_op jit(solution)/shard_map/ppermute | solution.py:9
  379.8 33.9 %collective-permute-start.6 = (bf16[3,128,768]{2,1,0:T(8,128)(2,1)}, bf16[3,128,768]{2,1,0:T(8,128)(2,1)}, u32[]{:S(2)}, u32[]{:S(2)}) collective-permute-start(bf16[3,128,768]{2,1,0:T(8,128)(2,1)} %pad_maximum_fusion.1), channel_id=1, source_target_pairs={{0,4},{1,5},{2,6},{3,7},{4,0},{5,1},{6,2},{7,3},{8,12},{9,13},{10,... | collective-permute-start | bytes 1769480 | tf_op jit(solution)/shard_map/ppermute | solution.py:9
  381.3 32.4 %collective-permute-start.7 = (bf16[3,128,768]{2,1,0:T(8,128)(2,1)}, bf16[3,128,768]{2,1,0:T(8,128)(2,1)}, u32[]{:S(2)}, u32[]{:S(2)}) collective-permute-start(bf16[3,128,768]{2,1,0:T(8,128)(2,1)} %pad_maximum_fusion.1), channel_id=1, source_target_pairs={{0,8},{1,9},{2,10},{3,11},{4,12},{5,13},{6,14},{7,15},{8,0},{9,1},... | collective-permute-start | bytes 1769480 | tf_op jit(solution)/shard_map/ppermute | solution.py:9
  384.0 3.1 collective-permute-start
  387.1 3.7 collective-permute-start.1
  390.8 11.5 %collective-permute-start.2 = (f32[128,16]{0,1:T(8,128)S(1)}, f32[128,16]{0,1:T(8,128)S(1)}, u32[]{:S(2)}, u32[]{:S(2)}) collective-permute-start(f32[128,16]{0,1:T(8,128)S(1)} %add.86), channel_id=1, source_target_pairs={{0,64},{16,80},{32,96},{48,112},{64,0},{80,16},{96,32},{112,48},{1... | collective-permute-start | bytes 24584 | tf_op jit(solution)/shard_map/ppermute | solution.py:9
  402.3 7.7 %collective-permute-start.3 = (f32[128,16]{0,1:T(8,128)S(1)}, f32[128,16]{0,1:T(8,128)S(1)}, u32[]{:S(2)}, u32[]{:S(2)}) collective-permute-start(f32[128,16]{0,1:T(8,128)S(1)} %add.87), channel_id=1, source_target_pairs={{0,128},{16,144},{32,160},{48,176},{64,192},{80,208},{96,224},{112... | collective-permute-start | bytes 24584 | tf_op jit(solution)/shard_map/ppermute | solution.py:9
  414.4 11.3 %all-to-all-start.6 = ((f32[16,128,16]{1,2,0:T(8,128)}), f32[16,128,16]{1,2,0:T(8,128)S(1)}, u32[]{:S(2)}, u32[]{:S(2)}) async-start(f32[16,128,16]{1,2,0:T(8,128)} %broadcast_in_dim.19), calls=%async_computation.7 | async-start | bytes 262144 | tf_op jit(solution)/shard_map/all_to_all | solution.py:15
  (10 other events, 27.0 us)
Sparse Core Ops, SparseCore 0:
  307.7 65.7 reduce-scatter.1
